TPU v7x, 32 devices: a whole 2x2x4 slice. The times are simulated.
32 devices in a mesh: groups: 2 (over y), corr: 4 (over z), filt: 2 (over x), pair: 2 (over core).
Axes of the slice: x: 2, y: 2, z: 4, core: 2. Of those that a mesh axis runs over, the one named last changes fastest.
Arguments:
- raw_rows: bfloat16 [4, 32, 3, 16384], P(('groups', 'pair'), 'filt', None, 'corr'), parts along dimension 0, may hold values from -6 to 6
- valid_counts: int32 [4, 32], P(('groups', 'pair'), 'filt'), parts along dimension 0, may hold values from 4096 to 16384
- taps: bfloat16 [64], replicated, may hold values from -0.75 to 0.75
- templates: bfloat16 [128, 225], P('corr'), may hold values from -6 to 6
- masks: int32 [128, 3, 32], replicated, may hold values 0 or 1
Outputs:
- stack: float32 [4, 128, 4096], P(('groups', 'pair'), 'corr', 'filt'), parts along dimension 0
There are 2 independent parts, one for each index of `groups`. A program takes and returns all parts, laid end to end along the dimension named above; an argument that names none is the same for every part. Nothing has to cross between parts.
All inputs are finite; a program needn't handle non-finite values.
Results may differ from a plain program's by a relative error of at most 0.0051.
Values may be sent and summed in bfloat16 or wider, within the bound.
No kernel may reach another device: no remote copies, remote signals or barrier semaphores. Data moves between devices by JAX's collectives and lax.ppermute only.
A program may use at most 192 MiB of HBM per device.

v0:
```python
import jax
import jax.numpy as jnp
from jax import lax
from jax.sharding import PartitionSpec as P

L = 75
TAPS = 64
DEC = 4


def from_behind(block, axis, distance):
    devices = range(lax.axis_size(axis))
    route = [(i - distance, i) for i in devices if i - distance in devices]
    return lax.ppermute(block, axis, route)


def scaled_rows(extended):
    station_count = extended.shape[0]
    width = extended.shape[2] - (L - 1)
    slices = jnp.stack([extended[:, :, lag : lag + width] for lag in range(L)], axis=2)
    energy = jnp.einsum("scjt,scjt->sct", slices, slices, preferred_element_type=jnp.float32)
    scaled = (slices / jnp.sqrt(jnp.maximum(energy, 1.0))[:, :, None, :]).astype(jnp.bfloat16)
    return scaled.reshape(station_count * 3 * L, width)


def template_weights(template_rows, mask_rows):
    count = template_rows.shape[0]
    stations = mask_rows.shape[2]
    shaped = template_rows.astype(jnp.float32).reshape(count, 3, L)
    norms = jnp.sqrt(jnp.sum(shaped * shaped, axis=2) + 1e-06)
    base = shaped / norms[:, :, None]
    chosen = jnp.transpose(mask_rows.astype(jnp.float32), (0, 2, 1))
    full = base[:, None, :, :] * chosen[:, :, :, None]
    return full.astype(jnp.bfloat16).reshape(count, stations * 3 * L)


def body(raw_rows, valid_counts, taps, templates, masks):
    samples = raw_rows[0]
    counts = valid_counts[0]
    local_stations = samples.shape[0]
    raw_width = samples.shape[2]
    corr_place = lax.axis_index("corr")
    corr_count = lax.axis_size("corr")
    filt_count = lax.axis_size("filt")
    template_all = masks.shape[0]
    group_size = masks.shape[2] // (corr_count * filt_count)
    sample_times = corr_place * raw_width + lax.iota(jnp.int32, raw_width)
    live = jnp.where(
        sample_times[None, None, :] < counts[:, None, None], samples, jnp.zeros_like(samples)
    )
    history = from_behind(live[:, :, raw_width - (TAPS - 1) :], "corr", 1)
    extended = jnp.concatenate([history, live], axis=2).reshape(
        local_stations * 3, 1, raw_width + TAPS - 1
    )
    kernel = taps[::-1].reshape(1, 1, TAPS)
    filtered = lax.conv_general_dilated(
        extended,
        kernel,
        (DEC,),
        "VALID",
        dimension_numbers=("NCH", "OIH", "NCH"),
        preferred_element_type=jnp.float32,
    )
    decimated = raw_width // DEC
    filtered = filtered.astype(jnp.bfloat16).reshape(local_stations, 3, decimated)
    moved = lax.all_to_all(
        lax.all_to_all(filtered, "corr", split_axis=0, concat_axis=2, tiled=True),
        "filt",
        split_axis=2,
        concat_axis=0,
        tiled=True,
    )
    following = from_behind(moved[:, :, : L - 1], "filt", -1)
    lagged = jnp.concatenate([moved, following], axis=2)
    block_width = moved.shape[2]
    split_masks = masks.reshape(template_all, 3, filt_count, corr_count, group_size)
    mine = lax.dynamic_slice_in_dim(split_masks, corr_place, 1, 3).reshape(
        template_all, 3, filt_count * group_size
    )
    scaled = scaled_rows(lagged)
    empty = jnp.zeros((template_all, block_width), jnp.float32)
    weights = template_weights(lax.all_gather(templates, "corr", axis=0, tiled=True), mine)
    partial_rows = jnp.dot(weights, scaled, preferred_element_type=jnp.float32)
    totals = lax.dynamic_update_slice_in_dim(empty, partial_rows, jnp.int32(0), 0)
    stacked = lax.psum_scatter(totals, "corr", scatter_dimension=0, tiled=True)
    return stacked[None]


def solution(mesh):
    return jax.shard_map(
        body,
        mesh=mesh,
        in_specs=(
            P(("groups", "pair"), "filt", None, "corr"),
            P(("groups", "pair"), "filt"),
            P(),
            P("corr", None),
            P(),
        ),
        out_specs=P(("groups", "pair"), "corr", "filt"),
        check_vma=False,
    )
```

profile of v0, /device:TPU:0, one launch (start us, length us, event | category | flops | bytes accessed | tf_op | source)
XLA Modules:
  0.0 146.4 jit_solution(11278841921117078168)
XLA Ops:
  6.5 0.8 broadcast_compare_fusion
  7.3 1.0 bitcast_select_fusion
  8.4 4.9 %collective-permute-start = (bf16[16,3,63]{2,0,1:T(8,128)(2,1)S(1)}, bf16[16,3,63]{2,0,1:T(8,128)(2,1)S(1)}, u32[]{:S(2)}, u32[]{:S(2)}) collective-permute-start(bf16[16,3,63]{2,0,1:T(8,128)(2,1)S(1)} %slice.304), channel_id=1, source_target_pairs={{0,4},{4,8},{8,12},{1,5},{5,9},{9,13},{2,6},{6,10},{10,14},{3,7},{... | collective-permute-start | bytes 18152 | tf_op jit(solution)/shard_map/ppermute | solution.py:14
  13.4 13.7 %all_gather.3 = bf16[128,225]{1,0:T(8,128)(2,1)S(1)} all-gather(bf16[32,225]{1,0:T(8,128)(2,1)} %param.8), channel_id=1, replica_groups=mesh['groups'=2,'corr'=4,'filt'=2,'pair'=2] {'corr'}, dimensions={0}, use_global_device_ids=true | all-gather | bytes 72000 | tf_op jit(solution)/shard_map/all_gather | solution.py:82
  27.1 0.1 copy.130
  27.3 0.7 rev.3
  28.0 0.1 copy.134
  28.1 0.2 pad_maximum_fusion
  28.3 0.2 copy.132
  28.5 0.3 reshape.73
  28.9 2.8 %copy.133 = bf16[48,1,4159]{0,1,2:T(2,128)(2,1)S(1)} copy(bf16[48,1,4159]{2,0,1:T(8,128)(2,1)S(1)} %reshape.73) | data formatting | bytes 798528 | tf_op jit(solution)/shard_map/reshape | solution.py:52
  31.7 11.7 %convolution_convert_fusion = bf16[48,1,1024]{0,1,2:T(2,128)(2,1)S(1)} fusion(bf16[48,1,4159]{0,1,2:T(2,128)(2,1)S(1)} %copy.133, bf16[1,1,64]{1,0,2:T(2,128)(2,1)S(1)} %copy.134), kind=kOutput, calls=%fused_computation.6 | convolution fusion | flops 6340608 | bytes 497696 | tf_op jit(solution)/shard_map/conv_general_dilated | solution.py:56
  43.4 0.3 copy.135
  43.7 0.7 reshape.75
  44.5 3.3 %all-to-all-start = ((bf16[16,3,1024]{2,1,0:T(4,128)(2,1)}), bf16[16,3,1024]{2,1,0:T(4,128)(2,1)S(1)}, u32[]{:S(2)}, u32[]{:S(2)}) async-start(bf16[16,3,1024]{2,1,0:T(4,128)(2,1)} %reshape.75), calls=%async_computation | async-start | bytes 262144 | tf_op jit(solution)/shard_map/all_to_all | solution.py:67
  47.8 5.9 %all-to-all-done = bf16[16,3,1024]{2,1,0:T(4,128)(2,1)S(1)} async-done(((bf16[16,3,1024]{2,1,0:T(4,128)(2,1)}), bf16[16,3,1024]{2,1,0:T(4,128)(2,1)S(1)}, u32[]{:S(2)}, u32[]{:S(2)}) %all-to-all-start) | async-done | bytes 98336 | tf_op jit(solution)/shard_map/all_to_all | solution.py:67
  53.7 4.7 %copy.149 = bf16[4,3,4,1024]{0,1,3,2:T(4,128)(2,1)} copy(bf16[4,3,4,1024]{3,1,0,2:T(4,128)(2,1)S(1)} %bitcast.336) | data formatting | bytes 196608 | tf_op jit(solution)/shard_map/all_to_all | solution.py:67
  58.4 5.8 %reshape.81 = bf16[2,2,12288]{2,1,0:T(2,128)(2,1)} reshape(bf16[4096,3,4]{2,1,0:T(4,128)(2,1)} %bitcast.334) | data formatting | bytes 196608
  64.3 3.3 %all-to-all-start.1 = ((bf16[2,2,12288]{2,1,0:T(2,128)(2,1)}), bf16[2,2,12288]{2,1,0:T(2,128)(2,1)S(1)}, u32[]{:S(2)}, u32[]{:S(2)}) async-start(bf16[2,2,12288]{2,1,0:T(2,128)(2,1)} %reshape.81), calls=%async_computation.1 | async-start | bytes 196608 | tf_op jit(solution)/shard_map/all_to_all | solution.py:66
  67.7 0.7 dynamic-slice_convert_fusion
  68.4 3.5 %all-to-all-done.1 = bf16[2,2,12288]{2,1,0:T(2,128)(2,1)S(1)} async-done(((bf16[2,2,12288]{2,1,0:T(2,128)(2,1)}), bf16[2,2,12288]{2,1,0:T(2,128)(2,1)S(1)}, u32[]{:S(2)}, u32[]{:S(2)}) %all-to-all-start.1) | async-done | bytes 98336 | tf_op jit(solution)/shard_map/all_to_all | solution.py:66
  71.9 5.1 %reshape.82 = bf16[4096,3,4]{2,1,0:T(4,128)(2,1)} reshape(bf16[2,2,12288]{2,1,0:T(2,128)(2,1)S(1)} %all-to-all-done.1) | data formatting | bytes 196608
  77.0 5.9 %copy.150 = bf16[4,3,2,2048]{3,2,0,1:T(2,128)(2,1)S(1)} copy(bf16[4,3,2,2048]{0,1,3,2:T(4,128)(2,1)} %bitcast.335) | data formatting | bytes 196608 | tf_op jit(solution)/shard_map/all_to_all | solution.py:66
  83.0 1.5 %collective-permute-start.1 = (bf16[8,3,74]{2,0,1:T(8,128)(2,1)S(1)}, bf16[8,3,74]{2,0,1:T(8,128)(2,1)S(1)}, u32[]{:S(2)}, u32[]{:S(2)}) collective-permute-start(bf16[8,3,74]{2,0,1:T(8,128)(2,1)S(1)} %slice.305), channel_id=1, source_target_pairs={{2,0},{3,1},{6,4},{7,5},{10,8},{11,9},{14,12},{15,13},{18,16},{19,... | collective-permute-start | bytes 10664 | tf_op jit(solution)/shard_map/ppermute | solution.py:14
  84.5 4.0 %collective-permute-done.1 = bf16[8,3,74]{2,0,1:T(8,128)(2,1)S(1)} collective-permute-done((bf16[8,3,74]{2,0,1:T(8,128)(2,1)S(1)}, bf16[8,3,74]{2,0,1:T(8,128)(2,1)S(1)}, u32[]{:S(2)}, u32[]{:S(2)}) %collective-permute-start.1) | collective-permute-done | bytes 3584 | tf_op jit(solution)/shard_map/ppermute | solution.py:14
  88.5 0.1 constant_dynamic-update-slice_fusion.75
  88.6 0.1 constant_dynamic-update-slice_fusion.74
  96.0 1.6 %fusion = f32[8,3,2048]{2,0,1:T(8,128)S(1)} fusion(bf16[8,3,75,2048]{3,0,1,2:T(8,128)(2,1)S(1)} %constant_dynamic-update-slice_fusion.2), kind=kLoop, calls=%fused_computation.1 | loop fusion | flops 11010048 | bytes 7569408 | tf_op jit(solution)/shard_map/scjt,scjt->sct/dot_general | solution.py:21
  97.6 1.4 copy-done
  99.0 5.3 %divide_convert_fusion = bf16[8,3,75,2048]{3,0,1,2:T(8,128)(2,1)S(1)} fusion(bf16[8,3,75,2048]{3,0,1,2:T(8,128)(2,1)} %copy-done, f32[8,3,2048]{2,0,1:T(8,128)S(1)} %maximum_sqrt_fusion), kind=kLoop, calls=%fused_computation.2 | loop fusion | flops 11059200 | bytes 14942208 | tf_op jit(solution)/shard_map/convert_element_type | solution.py:22
  104.3 9.6 %fusion.3 = f32[128,2048]{1,0:T(8,128)} fusion(bf16[8,3,75,2048]{3,0,1,2:T(8,128)(2,1)S(1)} %divide_convert_fusion, f32[128,8,3]{0,2,1:T(4,128)S(1)} %bitcast.338, f32[128,3,75]{0,2,1:T(8,128)S(1)} %broadcast_divide_fusion), kind=kOutput, calls=%fused_computation.5 | convolution fusion | flops 944179200 | bytes 8548864 | tf_op jit(solution)/shard_map/dot_general | solution.py:83
  113.9 25.6 %reduce-scatter.2.cloned.1.call-done = f32[32,2048]{1,0:T(8,128)} async-done(((f32[128,2048]{1,0:T(8,128)}), f32[32,2048]{1,0:T(8,128)}) %reduce-scatter.2.cloned.1.call-update) | async-done | bytes 262160 | tf_op jit(solution)/shard_map/reduce_scatter | solution.py:85
  (91 shorter events, 7.2 us)
Async XLA Ops:
  8.4 19.7 %collective-permute-start = (bf16[16,3,63]{2,0,1:T(8,128)(2,1)S(1)}, bf16[16,3,63]{2,0,1:T(8,128)(2,1)S(1)}, u32[]{:S(2)}, u32[]{:S(2)}) collective-permute-start(bf16[16,3,63]{2,0,1:T(8,128)(2,1)S(1)} %slice.304), channel_id=1, source_target_pairs={{0,4},{4,8},{8,12},{1,5},{5,9},{9,13},{2,6},{6,10},{10,14},{3,7},{... | collective-permute-start | bytes 18152 | tf_op jit(solution)/shard_map/ppermute | solution.py:14
  44.5 9.2 %all-to-all-start = ((bf16[16,3,1024]{2,1,0:T(4,128)(2,1)}), bf16[16,3,1024]{2,1,0:T(4,128)(2,1)S(1)}, u32[]{:S(2)}, u32[]{:S(2)}) async-start(bf16[16,3,1024]{2,1,0:T(4,128)(2,1)} %reshape.75), calls=%async_computation | async-start | bytes 262144 | tf_op jit(solution)/shard_map/all_to_all | solution.py:67
  64.3 7.6 %all-to-all-start.1 = ((bf16[2,2,12288]{2,1,0:T(2,128)(2,1)}), bf16[2,2,12288]{2,1,0:T(2,128)(2,1)S(1)}, u32[]{:S(2)}, u32[]{:S(2)}) async-start(bf16[2,2,12288]{2,1,0:T(2,128)(2,1)} %reshape.81), calls=%async_computation.1 | async-start | bytes 196608 | tf_op jit(solution)/shard_map/all_to_all | solution.py:66
  67.6 71.9 %reduce-scatter.2.cloned.1.call-start = ((), (), s32[]{:S(2)}) async-start(), calls=%async_computation.3 | async-start | bytes 1310720 | tf_op jit(solution)/shard_map/reduce_scatter | solution.py:85
  83.0 5.5 %collective-permute-start.1 = (bf16[8,3,74]{2,0,1:T(8,128)(2,1)S(1)}, bf16[8,3,74]{2,0,1:T(8,128)(2,1)S(1)}, u32[]{:S(2)}, u32[]{:S(2)}) collective-permute-start(bf16[8,3,74]{2,0,1:T(8,128)(2,1)S(1)} %slice.305), channel_id=1, source_target_pairs={{2,0},{3,1},{6,4},{7,5},{10,8},{11,9},{14,12},{15,13},{18,16},{19,... | collective-permute-start | bytes 10664 | tf_op jit(solution)/shard_map/ppermute | solution.py:14
  96.0 3.0 %copy-start = (bf16[8,3,75,2048]{3,0,1,2:T(8,128)(2,1)}, bf16[8,3,75,2048]{3,0,1,2:T(8,128)(2,1)S(1)}, u32[]{:S(2)}) copy-start(bf16[8,3,75,2048]{3,0,1,2:T(8,128)(2,1)S(1)} %constant_dynamic-update-slice_fusion.2) | copy-start | bytes 22118404
Sparse Core Ops, SparseCore 0:
  114.0 25.4 reduce-scatter.1
where the time goes:
time: 147 us; the launch traced here: 146 us
  waiting for transfers between devices  39 us (27%)
  local copies, waits for them, and re-layouts  35.5 us (24%)
  matrix products  21.2 us (14%)
  between operations  14.1 us (10%)
  blocking collectives  13.7 us (9%)
  starting transfers between devices  13.1 us (9%)
  other arithmetic  9.66 us (7%)
    reduce_scatter x1, waiting for transfers between devices, body(): stacked = lax.psum_scatter(totals, 'corr', scatter_dimension=0, tiled=True)  25.6 us
    unnamed x79, local copies, waits for them, and re-layouts  19.2 us
    all_gather x1, blocking collectives, body(): lax.all_gather(templates, 'corr', axis=0, tiled=True)  13.7 us
    conv_general_dilated x1, matrix products, body(): lax.conv_general_dilated(extended, kernel, (DEC,), 'VALID', dimension_num...  11.7 us
    dot_general x1, matrix products, body(): partial_rows = jnp.dot(weights, scaled, preferred_element_type=jnp.float32)  9.56 us
    ppermute x2, starting transfers between devices, from_behind(): return lax.ppermute(block, axis, route)  6.42 us
    all_to_all x3, local copies, waits for them, and re-layouts, body(): lax.all_to_all(lax.all_to_all(filtered, 'corr', split_axis=0, concat_axis...  5.94 us
    all_to_all x1, waiting for transfers between devices, body(): lax.all_to_all(filtered, 'corr', split_axis=0, concat_axis=2, tiled=True)  5.86 us
  transfers between devices with their start and end apart: 5, of which 4 were waited for; matrix products, arithmetic and copies ran while one was open for 1% of the time, Pallas kernels for 0%

commit v1 on v0

--- a/solution.py
+++ b/solution.py
@@ -6,6 +6,28 @@
 L = 75
 TAPS = 64
 DEC = 4
+
+
+def split_up(value, dim, size):
+    before, after = (value.shape[:dim], value.shape[dim + 1 :])
+    return jnp.moveaxis(value.reshape(*before, size, -1, *after), dim, 0)
+
+
+def in_order(pieces, dim):
+    shape = list(pieces.shape[1:])
+    shape[dim] *= pieces.shape[0]
+    return jnp.moveaxis(pieces, 0, dim).reshape(shape)
+
+
+def pairwise_exchange(x, axis, split_dim, concat_dim):
+    peers, index = (lax.axis_size(axis), lax.axis_index(axis))
+    blocks = split_up(x, split_dim, peers)
+    done = [blocks[index]]
+    for step in range(1, peers):
+        sent = blocks[index ^ step]
+        done.append(lax.ppermute(sent, axis, [(i, i ^ step) for i in range(peers)]))
+    blocks = jnp.stack(done)[index ^ jnp.arange(peers)]
+    return in_order(blocks, concat_dim)
 
 
 def from_behind(block, axis, distance):
@@ -64,11 +86,7 @@
     decimated = raw_width // DEC
     filtered = filtered.astype(jnp.bfloat16).reshape(local_stations, 3, decimated)
     moved = lax.all_to_all(
-        lax.all_to_all(filtered, "corr", split_axis=0, concat_axis=2, tiled=True),
-        "filt",
-        split_axis=2,
-        concat_axis=0,
-        tiled=True,
+        pairwise_exchange(filtered, "corr", 0, 2), "filt", split_axis=2, concat_axis=0, tiled=True
     )
     following = from_behind(moved[:, :, : L - 1], "filt", -1)
     lagged = jnp.concatenate([moved, following], axis=2)

time: 147 us -> 145 us (0.986)
  waiting for transfers between devices: 39 us -> 36.5 us
    all_to_all x2 -> x1, waiting for transfers between devices: 9.37 us -> 3.51 us  [body(): lax.all_to_all(pairwise_exchange(filtered, 'corr', 0, 2), 'filt', split_a...]
    all_to_all x4 -> x3, local copies, waits for them, and re-layouts: 10.7 us -> 5.94 us  [body(): lax.all_to_all(pairwise_exchange(filtered, 'corr', 0, 2), 'filt', split_a...]
    reshape x1, local copies, waits for them, and re-layouts: 0.73 us -> 4.76 us  [in_order(): return jnp.moveaxis(pieces, 0, dim).reshape(shape)]
    ppermute x0 -> x3, starting transfers between devices: none -> 3.55 us  [pairwise_exchange(): done.append(lax.ppermute(sent, axis, [(i, i ^ step) for i in range(peers)]))]
    all_to_all x2 -> x1, starting transfers between devices: 6.66 us -> 3.34 us  [body(): lax.all_to_all(pairwise_exchange(filtered, 'corr', 0, 2), 'filt', split_a...]
    ppermute x0 -> x3, waiting for transfers between devices: none -> 2.8 us  [pairwise_exchange(): done.append(lax.ppermute(sent, axis, [(i, i ^ step) for i in range(peers)]))]
  transfers between devices with their start and end apart: 5 -> 7, of which waited for: 4 -> 5; matrix products, arithmetic and copies ran while one was open for 1% -> 1% of each run, Pallas kernels for 0% -> 0%
where the time goes in v1:
time: 145 us; the launch traced here: 144 us
  waiting for transfers between devices  36.5 us (25%)
  local copies, waits for them, and re-layouts  35.6 us (25%)
  matrix products  21.2 us (15%)
  between operations  14.1 us (10%)
  blocking collectives  13.7 us (9%)
  starting transfers between devices  13.3 us (9%)
  other arithmetic  9.79 us (7%)
    reduce_scatter x1, waiting for transfers between devices, body(): stacked = lax.psum_scatter(totals, 'corr', scatter_dimension=0, tiled=True)  26.2 us
    unnamed x79, local copies, waits for them, and re-layouts  19.2 us
    all_gather x1, blocking collectives, body(): lax.all_gather(templates, 'corr', axis=0, tiled=True)  13.7 us
    conv_general_dilated x1, matrix products, body(): lax.conv_general_dilated(extended, kernel, (DEC,), 'VALID', dimension_num...  11.7 us
    dot_general x1, matrix products, body(): partial_rows = jnp.dot(weights, scaled, preferred_element_type=jnp.float32)  9.56 us
    ppermute x2, starting transfers between devices, from_behind(): return lax.ppermute(block, axis, route)  6.42 us
    all_to_all x3, local copies, waits for them, and re-layouts, body(): lax.all_to_all(pairwise_exchange(filtered, 'corr', 0, 2), 'filt', split_a...  5.94 us
    convert_element_type x1, other arithmetic, scaled_rows(): (slices / jnp.sqrt(jnp.maximum(energy, 1.0))[:, :, None, :]).astype(jnp.b...  5.31 us
  transfers between devices with their start and end apart: 7, of which 5 were waited for; matrix products, arithmetic and copies ran while one was open for 1% of the time, Pallas kernels for 0%

profile of v1, /device:TPU:0, one launch (start us, length us, event | category | flops | bytes accessed | tf_op | source)
XLA Modules:
  0.0 144.4 jit_solution(7350421874374603610)
XLA Ops:
  6.5 0.8 broadcast_compare_fusion
  7.3 1.0 bitcast_select_fusion
  8.4 4.9 %collective-permute-start = (bf16[16,3,63]{2,0,1:T(8,128)(2,1)S(1)}, bf16[16,3,63]{2,0,1:T(8,128)(2,1)S(1)}, u32[]{:S(2)}, u32[]{:S(2)}) collective-permute-start(bf16[16,3,63]{2,0,1:T(8,128)(2,1)S(1)} %slice.306), channel_id=1, source_target_pairs={{0,4},{4,8},{8,12},{1,5},{5,9},{9,13},{2,6},{6,10},{10,14},{3,7},{... | collective-permute-start | bytes 18152 | tf_op jit(solution)/shard_map/ppermute | solution.py:36
  13.4 13.7 %all_gather.3 = bf16[128,225]{1,0:T(8,128)(2,1)S(1)} all-gather(bf16[32,225]{1,0:T(8,128)(2,1)} %param.8), channel_id=1, replica_groups=mesh['groups'=2,'corr'=4,'filt'=2,'pair'=2] {'corr'}, dimensions={0}, use_global_device_ids=true | all-gather | bytes 72000 | tf_op jit(solution)/shard_map/all_gather | solution.py:100
  27.3 0.7 rev.3
  28.1 0.1 copy.133
  28.2 0.2 pad_maximum_fusion
  28.4 0.2 copy.131
  28.6 0.3 reshape.89
  29.0 2.8 %copy.132 = bf16[48,1,4159]{0,1,2:T(2,128)(2,1)S(1)} copy(bf16[48,1,4159]{2,0,1:T(8,128)(2,1)S(1)} %reshape.89) | data formatting | bytes 798528 | tf_op jit(solution)/shard_map/reshape | solution.py:74
  31.8 11.7 %convolution_convert_fusion = bf16[48,1,1024]{0,1,2:T(2,128)(2,1)S(1)} fusion(bf16[48,1,4159]{0,1,2:T(2,128)(2,1)S(1)} %copy.132, bf16[1,1,64]{1,0,2:T(2,128)(2,1)S(1)} %copy.133), kind=kOutput, calls=%fused_computation.7 | convolution fusion | flops 6340608 | bytes 497696 | tf_op jit(solution)/shard_map/conv_general_dilated | solution.py:78
  43.5 0.3 copy.134
  44.0 0.6 collective-permute-start.2
  44.6 1.2 collective-permute-start.3
  45.8 1.7 %collective-permute-start.1 = (bf16[4,3,1024]{2,1,0:T(4,128)(2,1)S(1)}, bf16[4,3,1024]{2,1,0:T(4,128)(2,1)S(1)}, u32[]{:S(2)}, u32[]{:S(2)}) collective-permute-start(bf16[4,3,1024]{2,1,0:T(4,128)(2,1)S(1)} %get-tuple-element.8), channel_id=1, source_target_pairs={{0,4},{4,0},{8,12},{12,8},{1,5},{5,1},{9,13},{13,9},{2,6},{6,2},{1... | collective-permute-start | bytes 73736 | tf_op jit(solution)/shard_map/ppermute | solution.py:28
  47.5 1.3 collective-permute-done.2
  48.8 1.5 %collective-permute-done.3 = bf16[4,3,1024]{2,1,0:T(4,128)(2,1)S(1)} collective-permute-done((bf16[4,3,1024]{2,1,0:T(4,128)(2,1)S(1)}, bf16[4,3,1024]{2,1,0:T(4,128)(2,1)S(1)}, u32[]{:S(2)}, u32[]{:S(2)}) %collective-permute-start.3) | collective-permute-done | bytes 24608 | tf_op jit(solution)/shard_map/ppermute | solution.py:28
  50.4 0.7 gather_fusion
  51.1 4.8 %copy.148 = bf16[4,3,4,1024]{0,1,3,2:T(4,128)(2,1)} copy(bf16[4,3,4,1024]{3,1,0,2:T(4,128)(2,1)S(1)} %bitcast.344) | data formatting | bytes 196608 | tf_op jit(solution)/shard_map/reshape | solution.py:19
  55.9 5.8 %reshape.105 = bf16[2,2,12288]{2,1,0:T(2,128)(2,1)} reshape(bf16[4096,3,4]{2,1,0:T(4,128)(2,1)} %bitcast.342) | data formatting | bytes 196608
  61.7 3.3 %all-to-all-start = ((bf16[2,2,12288]{2,1,0:T(2,128)(2,1)}), bf16[2,2,12288]{2,1,0:T(2,128)(2,1)S(1)}, u32[]{:S(2)}, u32[]{:S(2)}) async-start(bf16[2,2,12288]{2,1,0:T(2,128)(2,1)} %reshape.105), calls=%async_computation | async-start | bytes 196608 | tf_op jit(solution)/shard_map/all_to_all | solution.py:88
  65.1 0.7 dynamic-slice_convert_fusion
  65.8 3.5 %all-to-all-done = bf16[2,2,12288]{2,1,0:T(2,128)(2,1)S(1)} async-done(((bf16[2,2,12288]{2,1,0:T(2,128)(2,1)}), bf16[2,2,12288]{2,1,0:T(2,128)(2,1)S(1)}, u32[]{:S(2)}, u32[]{:S(2)}) %all-to-all-start) | async-done | bytes 98336 | tf_op jit(solution)/shard_map/all_to_all | solution.py:88
  69.3 5.1 %reshape.106 = bf16[4096,3,4]{2,1,0:T(4,128)(2,1)} reshape(bf16[2,2,12288]{2,1,0:T(2,128)(2,1)S(1)} %all-to-all-done) | data formatting | bytes 196608
  74.4 5.9 %copy.149 = bf16[4,3,2,2048]{3,2,0,1:T(2,128)(2,1)S(1)} copy(bf16[4,3,2,2048]{0,1,3,2:T(4,128)(2,1)} %bitcast.343) | data formatting | bytes 196608 | tf_op jit(solution)/shard_map/all_to_all | solution.py:88
  80.4 1.5 %collective-permute-start.4 = (bf16[8,3,74]{2,0,1:T(8,128)(2,1)S(1)}, bf16[8,3,74]{2,0,1:T(8,128)(2,1)S(1)}, u32[]{:S(2)}, u32[]{:S(2)}) collective-permute-start(bf16[8,3,74]{2,0,1:T(8,128)(2,1)S(1)} %slice.307), channel_id=1, source_target_pairs={{2,0},{3,1},{6,4},{7,5},{10,8},{11,9},{14,12},{15,13},{18,16},{19,... | collective-permute-start | bytes 10664 | tf_op jit(solution)/shard_map/ppermute | solution.py:36
  81.9 4.0 %collective-permute-done.4 = bf16[8,3,74]{2,0,1:T(8,128)(2,1)S(1)} collective-permute-done((bf16[8,3,74]{2,0,1:T(8,128)(2,1)S(1)}, bf16[8,3,74]{2,0,1:T(8,128)(2,1)S(1)}, u32[]{:S(2)}, u32[]{:S(2)}) %collective-permute-start.4) | collective-permute-done | bytes 3584 | tf_op jit(solution)/shard_map/ppermute | solution.py:36
  93.5 1.6 %fusion = f32[8,3,2048]{2,0,1:T(8,128)S(1)} fusion(bf16[8,3,75,2048]{3,0,1,2:T(8,128)(2,1)S(1)} %constant_dynamic-update-slice_fusion.2), kind=kLoop, calls=%fused_computation.2 | loop fusion | flops 11010048 | bytes 7569408 | tf_op jit(solution)/shard_map/scjt,scjt->sct/dot_general | solution.py:43
  95.0 1.4 copy-done
  96.5 5.3 %divide_convert_fusion = bf16[8,3,75,2048]{3,0,1,2:T(8,128)(2,1)S(1)} fusion(bf16[8,3,75,2048]{3,0,1,2:T(8,128)(2,1)} %copy-done, f32[8,3,2048]{2,0,1:T(8,128)S(1)} %maximum_sqrt_fusion), kind=kLoop, calls=%fused_computation.3 | loop fusion | flops 11059200 | bytes 14942208 | tf_op jit(solution)/shard_map/convert_element_type | solution.py:44
  101.8 9.6 %fusion.3 = f32[128,2048]{1,0:T(8,128)} fusion(bf16[8,3,75,2048]{3,0,1,2:T(8,128)(2,1)S(1)} %divide_convert_fusion, f32[128,8,3]{0,2,1:T(4,128)S(1)} %bitcast.346, f32[128,3,75]{0,2,1:T(8,128)S(1)} %broadcast_divide_fusion), kind=kOutput, calls=%fused_computation.6 | convolution fusion | flops 944179200 | bytes 8548864 | tf_op jit(solution)/shard_map/dot_general | solution.py:101
  111.4 26.2 %reduce-scatter.2.cloned.1.call-done = f32[32,2048]{1,0:T(8,128)} async-done(((f32[128,2048]{1,0:T(8,128)}), f32[32,2048]{1,0:T(8,128)}) %reduce-scatter.2.cloned.1.call-update) | async-done | bytes 262160 | tf_op jit(solution)/shard_map/reduce_scatter | solution.py:103
  (100 shorter events, 7.8 us)
Async XLA Ops:
  8.4 19.8 %collective-permute-start = (bf16[16,3,63]{2,0,1:T(8,128)(2,1)S(1)}, bf16[16,3,63]{2,0,1:T(8,128)(2,1)S(1)}, u32[]{:S(2)}, u32[]{:S(2)}) collective-permute-start(bf16[16,3,63]{2,0,1:T(8,128)(2,1)S(1)} %slice.306), channel_id=1, source_target_pairs={{0,4},{4,8},{8,12},{1,5},{5,9},{9,13},{2,6},{6,10},{10,14},{3,7},{... | collective-permute-start | bytes 18152 | tf_op jit(solution)/shard_map/ppermute | solution.py:36
  44.0 4.9 %collective-permute-start.2 = (bf16[4,3,1024]{2,1,0:T(4,128)(2,1)S(1)}, bf16[4,3,1024]{2,1,0:T(4,128)(2,1)S(1)}, u32[]{:S(2)}, u32[]{:S(2)}) collective-permute-start(bf16[4,3,1024]{2,1,0:T(4,128)(2,1)S(1)} %get-tuple-element.7), channel_id=1, source_target_pairs={{0,8},{4,12},{8,0},{12,4},{1,9},{5,13},{9,1},{13,5},{2,10},{6,14},... | collective-permute-start | bytes 73736 | tf_op jit(solution)/shard_map/ppermute | solution.py:28
  44.6 5.7 %collective-permute-start.3 = (bf16[4,3,1024]{2,1,0:T(4,128)(2,1)S(1)}, bf16[4,3,1024]{2,1,0:T(4,128)(2,1)S(1)}, u32[]{:S(2)}, u32[]{:S(2)}) collective-permute-start(bf16[4,3,1024]{2,1,0:T(4,128)(2,1)S(1)} %get-tuple-element.6), channel_id=1, source_target_pairs={{0,12},{4,8},{8,4},{12,0},{1,13},{5,9},{9,5},{13,1},{2,14},{6,10},... | collective-permute-start | bytes 73736 | tf_op jit(solution)/shard_map/ppermute | solution.py:28
  45.8 4.5 %collective-permute-start.1 = (bf16[4,3,1024]{2,1,0:T(4,128)(2,1)S(1)}, bf16[4,3,1024]{2,1,0:T(4,128)(2,1)S(1)}, u32[]{:S(2)}, u32[]{:S(2)}) collective-permute-start(bf16[4,3,1024]{2,1,0:T(4,128)(2,1)S(1)} %get-tuple-element.8), channel_id=1, source_target_pairs={{0,4},{4,0},{8,12},{12,8},{1,5},{5,1},{9,13},{13,9},{2,6},{6,2},{1... | collective-permute-start | bytes 73736 | tf_op jit(solution)/shard_map/ppermute | solution.py:28
  61.7 7.6 %all-to-all-start = ((bf16[2,2,12288]{2,1,0:T(2,128)(2,1)}), bf16[2,2,12288]{2,1,0:T(2,128)(2,1)S(1)}, u32[]{:S(2)}, u32[]{:S(2)}) async-start(bf16[2,2,12288]{2,1,0:T(2,128)(2,1)} %reshape.105), calls=%async_computation | async-start | bytes 196608 | tf_op jit(solution)/shard_map/all_to_all | solution.py:88
  65.1 72.5 %reduce-scatter.2.cloned.1.call-start = ((), (), s32[]{:S(2)}) async-start(), calls=%async_computation.2 | async-start | bytes 1310720 | tf_op jit(solution)/shard_map/reduce_scatter | solution.py:103
  80.4 5.5 %collective-permute-start.4 = (bf16[8,3,74]{2,0,1:T(8,128)(2,1)S(1)}, bf16[8,3,74]{2,0,1:T(8,128)(2,1)S(1)}, u32[]{:S(2)}, u32[]{:S(2)}) collective-permute-start(bf16[8,3,74]{2,0,1:T(8,128)(2,1)S(1)} %slice.307), channel_id=1, source_target_pairs={{2,0},{3,1},{6,4},{7,5},{10,8},{11,9},{14,12},{15,13},{18,16},{19,... | collective-permute-start | bytes 10664 | tf_op jit(solution)/shard_map/ppermute | solution.py:36
  93.4 3.0 %copy-start = (bf16[8,3,75,2048]{3,0,1,2:T(8,128)(2,1)}, bf16[8,3,75,2048]{3,0,1,2:T(8,128)(2,1)S(1)}, u32[]{:S(2)}) copy-start(bf16[8,3,75,2048]{3,0,1,2:T(8,128)(2,1)S(1)} %constant_dynamic-update-slice_fusion.2) | copy-start | bytes 22118404
Sparse Core Ops, SparseCore 0:
  111.5 26.0 reduce-scatter.1
